TPU v7x, 32 devices: a whole 2x2x4 slice. The times are simulated.
32 devices in a mesh: dp: 8 (over z, core), mask: 4 (over y, x).
Axes of the slice: x: 2, y: 2, z: 4, core: 2. Of those that a mesh axis runs over, the one named last changes fastest.
Arguments:
- patches: bfloat16 [2048, 768], P(('dp', 'mask')), parts along dimension 0
- visible_index: int32 [32, 51], P('dp'), parts along dimension 0, may hold values from 0 to 255, as said below
- embed_w: bfloat16 [768, 1024], replicated
- w_qkv: bfloat16 [1024, 3072], replicated, may hold values from -0.1875 to 0.1875
- w_out: bfloat16 [1024, 1024], replicated, may hold values from -0.1875 to 0.1875
- mask_embed: bfloat16 [1024], replicated, may hold values from -4 to 4
- dec_in: bfloat16 [1024, 768], replicated, may hold values from -0.1875 to 0.1875
- conv_w: bfloat16 [3, 16, 48, 48], replicated, may hold values from -0.5 to 0.5
- dec_out: bfloat16 [768, 1024], replicated, may hold values from -0.21875 to 0.21875
Outputs:
- embed_grad: float32 [6144, 1024], P(('dp', 'mask')), parts along dimension 0
- copy_loss: float32 [32], P(('dp', 'mask')), parts along dimension 0
There are 8 independent parts, one for each index of `dp`. A program takes and returns all parts, laid end to end along the dimension named above; an argument that names none is the same for every part. Nothing has to cross between parts.
Inputs may be any that keep to these rules, and one draw needn't show every extreme that they name: `visible_index`: each row lists 51 different patches; among the 64 patches of one index of mask (patches k * 64 to (k + 1) * 64 - 1) a row lists at most 26, and in every row some index's patches reach 26.
All inputs are finite; a program needn't handle non-finite values.
Results may differ from a plain program's by a relative error of at most 0.02.
Values may be sent and summed in bfloat16 or wider, within the bound.
No kernel may reach another device: no remote copies, remote signals or barrier semaphores. Data moves between devices by JAX's collectives and lax.ppermute only.
A program may use at most 128 MiB of HBM per device.

v0:
```python
import math
import jax
import jax.numpy as jnp
from jax import lax
from jax.sharding import PartitionSpec as P

D = 1024
HEADS = 16
DD = 768
GROUPS = 16
EPSILON = 1e-06


def row_norm(values):
    average = jnp.mean(values, axis=-1, keepdims=True)
    centred = values - average
    spread = jnp.mean(centred * centred, axis=-1, keepdims=True)
    return centred * lax.rsqrt(spread + EPSILON)


def head_norm(values):
    return values * lax.rsqrt(jnp.mean(values * values, axis=-1, keepdims=True) + EPSILON)


def mix_heads(queries, key_rows, values):
    score_scale = 1.0 / math.sqrt(queries.shape[-1])
    scores = (
        jnp.einsum("qhd,khd->hqk", queries, key_rows, preferred_element_type=jnp.float32)
        * score_scale
    )
    exponent = jnp.exp(scores)
    weights = (exponent / jnp.sum(exponent, axis=-1, keepdims=True)).astype(jnp.bfloat16)
    mixed = jnp.einsum("hqk,khd->qhd", weights, values, preferred_element_type=jnp.float32)
    return mixed.astype(jnp.bfloat16)


def split_project(projected):
    queries = head_norm(projected[:, 0].astype(jnp.float32)).astype(jnp.bfloat16)
    key_rows = head_norm(projected[:, 1].astype(jnp.float32)).astype(jnp.bfloat16)
    return mix_heads(queries, key_rows, projected[:, 2])


def attention_branch(inputs, w_qkv, w_out):
    row_count = inputs.shape[0]
    normed = row_norm(inputs.astype(jnp.float32)).astype(jnp.bfloat16)
    projected = jnp.dot(normed, w_qkv, preferred_element_type=jnp.float32).astype(jnp.bfloat16)
    context = split_project(projected.reshape(row_count, 3, HEADS, D // HEADS))
    return jnp.dot(context.reshape(row_count, D), w_out, preferred_element_type=jnp.float32)


def decoder_output(visible_out, positions, total_rows, mask_embed, dec_in, conv_w, dec_out):
    canvas = jnp.broadcast_to(mask_embed, (total_rows, D)).at[positions].set(visible_out)
    lowered = jnp.dot(canvas, dec_in, preferred_element_type=jnp.float32).astype(jnp.bfloat16)
    grouped = lowered.reshape(total_rows, GROUPS, DD // GROUPS)
    padded = jnp.pad(grouped, ((1, 1), (0, 0), (0, 0)))
    convolved = jnp.zeros((total_rows, GROUPS, DD // GROUPS), jnp.float32)
    for offset in range(3):
        convolved = convolved + jnp.einsum(
            "pgi,gio->pgo",
            padded[offset : offset + total_rows],
            conv_w[offset],
            preferred_element_type=jnp.float32,
        )
    activated = jax.nn.gelu(row_norm(convolved.reshape(total_rows, DD)), approximate=False)
    hidden = (lowered.astype(jnp.float32) + activated).astype(jnp.bfloat16)
    return jnp.dot(hidden, dec_out, preferred_element_type=jnp.float32)


def copy_terms(visible_in, positions, targets, w_qkv, w_out, mask_embed, dec_in, conv_w, dec_out):
    total_rows = targets.shape[0]
    visible_out = (
        visible_in.astype(jnp.float32) + attention_branch(visible_in, w_qkv, w_out)
    ).astype(jnp.bfloat16)
    predicted = decoder_output(
        visible_out, positions, total_rows, mask_embed, dec_in, conv_w, dec_out
    )
    slot_ids = jnp.arange(total_rows, dtype=jnp.int32)
    seen = jnp.max((slot_ids[:, None] == positions[None, :]).astype(jnp.float32), axis=1)
    mismatch = (predicted - targets.astype(jnp.float32)) * (1.0 - seen)[:, None]
    return jnp.sum(mismatch * mismatch)


def on_device(patches, visible_index, embed_w, w_qkv, w_out, mask_embed, dec_in, conv_w, dec_out):
    tok_rows = patches.shape[0]
    group_size = lax.axis_size("mask")
    own_index = lax.axis_index("mask")
    head_dim = D // HEADS
    heads_here = HEADS // group_size
    head_width = heads_here * head_dim
    copies = visible_index.shape[0]
    visible_count = visible_index.shape[1]
    total_rows = tok_rows * group_size
    positions = lax.dynamic_index_in_dim(visible_index, own_index, 0, keepdims=False)
    own_embedded = jnp.dot(patches, embed_w, preferred_element_type=jnp.float32).astype(
        jnp.bfloat16
    )
    embedded, clip_pixels = (
        lax.all_gather(own_embedded, "mask", axis=0, tiled=True),
        lax.all_gather(patches, "mask", axis=0, tiled=True),
    )
    visible_in = embedded[positions]
    normed = row_norm(embedded.astype(jnp.float32)).astype(jnp.bfloat16)
    own_cols = lax.dynamic_slice_in_dim(
        w_qkv.reshape(D, 3, D), own_index * head_width, head_width, 2
    )
    projected = jnp.einsum(
        "sd,dtw->stw", normed, own_cols, preferred_element_type=jnp.float32
    ).astype(jnp.bfloat16)
    context = split_project(projected.reshape(total_rows, 3, heads_here, head_dim))
    out_rows = lax.dynamic_slice_in_dim(w_out, own_index * head_width, head_width, 0)
    partial_value = jnp.dot(
        context.reshape(total_rows, head_width), out_rows, preferred_element_type=jnp.float32
    )
    branch = lax.psum(partial_value.astype(jnp.bfloat16), "mask").astype(jnp.float32)
    all_targets = row_norm(branch).astype(jnp.bfloat16)

    def objective(rows_in):
        return copy_terms(
            rows_in, positions, all_targets, w_qkv, w_out, mask_embed, dec_in, conv_w, dec_out
        )

    squares, pullback = jax.vjp(objective, visible_in)
    factor = 0.5 / math.sqrt(copies * visible_count)
    (grad_in,) = pullback(jnp.ones_like(squares) * factor)
    copy_loss = jnp.reshape(squares / ((total_rows - visible_count) * D), (1,))
    own_cols = lax.all_to_all(patches, "mask", split_axis=1, concat_axis=0, tiled=True)
    flat_index = visible_index.reshape(copies * visible_count)
    gathered = own_cols[flat_index]
    embed_grad = jnp.einsum(
        "vc,vd->cd",
        gathered,
        lax.all_gather(grad_in, "mask", axis=0, tiled=True),
        preferred_element_type=jnp.float32,
    )
    return (embed_grad, copy_loss)


def solution(mesh):
    placed = (P(("dp", "mask"), None), P("dp", None), P(), P(), P(), P(), P(), P(), P())
    return jax.shard_map(
        on_device,
        mesh=mesh,
        in_specs=placed,
        out_specs=(P(("dp", "mask"), None), P(("dp", "mask"))),
        check_vma=False,
    )
```

profile of v0, /device:TPU:0, one launch (start us, length us, event | category | flops | bytes accessed | tf_op | source)
XLA Modules:
  0.0 134.3 jit_solution(9758933965294009839)
XLA Ops:
  7.2 2.0 %convolution_convert_fusion.14 = bf16[64,1024]{1,0:T(8,128)(2,1)S(1)} fusion(bf16[64,768]{1,0:T(8,128)(2,1)} %param.9, bf16[768,1024]{1,0:T(8,128)(2,1)} %param.11), kind=kOutput, calls=%fused_computation.52 | convolution fusion | flops 100728832 | bytes 1802240 | tf_op jit(solution)/shard_map/dot_general | solution.py:94
  9.2 11.5 %all_gather.6 = bf16[256,1024]{1,0:T(8,128)(2,1)S(1)} all-gather(bf16[64,1024]{1,0:T(8,128)(2,1)S(1)} %convolution_convert_fusion.14), channel_id=1, replica_groups=mesh['dp'=8,'mask'=4] {'mask'}, dimensions={0}, use_global_device_ids=true | all-gather | bytes 655360 | tf_op jit(solution)/shard_map/all_gather | solution.py:98
  21.2 8.7 %copy.84 = bf16[1024,3072]{0,1:T(8,128)(2,1)} copy(bf16[1024,3072]{1,0:T(8,128)(2,1)} %param.12) | data formatting | bytes 12582912 | tf_op args[3]
  29.9 2.1 %fusion.4 = bf16[256,3,256]{0,2,1:T(8,128)(2,1)S(1)} fusion(bf16[1024,3,1024]{0,2,1:T(8,128)(2,1)} %bitcast.173, s32[]{:T(128)S(6)} %select_n.51, bf16[256,1024]{1,0:T(8,128)(2,1)S(1)} %all_gather.6, f32[256]{0:T(256)S(1)} %add_rsqrt_fusion.3, f32[256]{0:T(256)S(1)} %broadcast_multiply_fusion.2), kind=kOutput, calls=%fused_computation.21 | convolution fusion | flops 403898368 | bytes 2492420 | tf_op jit(solution)/shard_map/sd,dtw->stw/dot_general | solution.py:106
  32.1 1.3 %fusion.2 = f32[4,256,256]{1,2,0:T(8,128)} fusion(f32[256,4]{0,1:T(4,128)S(1)} %get-tuple-element.31, f32[256,4]{0,1:T(4,128)S(1)} %get-tuple-element.32, bf16[256,3,4,64]{0,3,2,1:T(8,128)(2,1)S(1)} %bitcast.182), kind=kOutput, calls=%fused_computation.10 | convolution fusion | flops 34209792 | bytes 1318912 | tf_op jit(solution)/shard_map/qhd,khd->hqk/dot_general | solution.py:28
  33.4 1.8 %convolution_convert_fusion.13 = bf16[4,64,256]{2,1,0:T(8,128)(2,1)S(1)} fusion(f32[4,256,256]{1,2,0:T(8,128)} %fusion.2, bf16[256,3,4,64]{0,3,2,1:T(8,128)(2,1)S(1)} %bitcast.183), kind=kOutput, calls=%fused_computation.51 | convolution fusion | flops 34145536 | bytes 2359296 | tf_op jit(solution)/shard_map/hqk,khd->qhd/dot_general | solution.py:33
  37.3 3.3 %all-to-all-start = ((bf16[64,4,192]{2,0,1:T(8,128)(2,1)}), bf16[64,4,192]{2,0,1:T(8,128)(2,1)S(1)}, u32[]{:S(2)}, u32[]{:S(2)}) async-start(bf16[64,4,192]{2,0,1:T(8,128)(2,1)} %copy.73), calls=%async_computation | async-start | bytes 262144 | tf_op jit(solution)/shard_map/all_to_all | solution.py:126
  43.2 4.0 %convolution_convert_fusion = bf16[51,3072]{1,0:T(8,128)(2,1)S(1)} fusion(bf16[1024,3072]{1,0:T(8,128)(2,1)} %param.12, bf16[51,1024]{1,0:T(8,128)(2,1)S(1)} %gather_fusion.2, f32[51]{0:T(128)S(1)} %fusion.116, f32[51]{0:T(128)S(1)} %broadcast_multiply_fusion.4), kind=kOutput, calls=%fused_computation.6 | convolution fusion | flops 321229824 | bytes 6709656 | tf_op jit(solution)/shard_map/jvp()/dot_general | solution.py:46
  51.0 1.3 gather_fusion.1
  55.4 1.5 %scatter_fusion = bf16[256,1024]{1,0:T(8,128)(2,1)S(1)} fusion(bf16[256,1024]{1,0:T(8,128)(2,1)S(1)} %copy-done.1, s32[51]{0:T(128)S(1)} %fusion.115, bf16[51,1024]{1,0:T(8,128)(2,1)S(1)} %fusion.24), kind=kCustom, calls=%fused_computation.5 | custom fusion | flops 52224 | bytes 313548 | tf_op jit(solution)/shard_map/jvp()/scatter-add | solution.py:52
  56.9 2.7 %convolution_convert_fusion.7 = bf16[256,768]{1,0:T(8,128)(2,1)} fusion(bf16[256,1024]{1,0:T(8,128)(2,1)S(1)} %scatter_fusion, bf16[1024,768]{1,0:T(8,128)(2,1)} %param.15), kind=kOutput, calls=%fused_computation.26 | convolution fusion | flops 402849792 | bytes 2490368 | tf_op jit(solution)/shard_map/jvp()/dot_general | solution.py:53
  60.8 1.3 fusion.62
  63.4 1.4 %fusion.128 = (f32[256]{0:T(256)S(1)}, f32[16,256,48]{1,2,0:T(8,128)S(1)}) fusion(f32[16,256,48]{1,2,0:T(8,128)S(1)} %convolution_add_fusion.1, bf16[256,16,48]{0,2,1:T(8,128)(2,1)S(1)} %bitcast.179, bf16[3,16,48,48]{3,2,1,0:T(8,128)(2,1)} %param.16), kind=kOutput, calls=%fused_computation.234 | convolution fusion | flops 19267328 | bytes 2163712 | tf_op jit(solution)/shard_map/jvp(pgi,gio->pgo)/dot_general | solution.py:58
  68.7 1.3 multiply_divide_fusion
  70.6 1.8 %gather_fusion = bf16[204,192]{1,0:T(8,128)(2,1)} fusion(bf16[256,192]{1,0:T(8,128)(2,1)S(1)} %bitcast.171, s32[1024]{0:T(1024)} %pad_clamp_fusion.1), kind=kCustom, calls=%fused_computation | custom fusion | bytes 157488 | tf_op jit(solution)/shard_map/gather | solution.py:128
  72.4 10.7 %all-reduce.9.cloned.1.call-done = bf16[256,1024]{1,0:T(8,128)(2,1)} async-done(((bf16[256,1024]{1,0:T(8,128)(2,1)}), bf16[256,1024]{1,0:T(8,128)(2,1)}) %all-reduce.9.cloned.1.call-update) | async-done | bytes 524304 | tf_op jit(solution)/shard_map/psum | solution.py:114
  84.3 1.3 fusion.25
  85.7 4.8 %multiply_reduce_fusion = (f32[]{:T(128)}, f32[256,1024]{1,0:T(8,128)S(1)}) fusion(f32[256]{0:T(256)} %get-tuple-element.12, f32[256]{0:T(256)S(1)} %add_rsqrt_fusion.2, f32[256]{0:T(256)S(1)} %broadcast_multiply_fusion.1, bf16[256,1024]{1,0:T(8,128)(2,1)} %all-reduce.9.cloned.1.call-done, bf16[768,1024]{1,0:T(8,128)(2,1)} %param.17, ...), kind=kOutput, calls=%fused_computation.64 | convolution fusion | flops 418971648 | bytes 4330500 | tf_op jit(solution)/shard_map/jvp()/dot_general | solution.py:66
  90.5 3.5 %multiply_reduce_fusion.1 = (f32[256]{0:T(256)S(1)}, bf16[256,768]{1,0:T(8,128)(2,1)S(1)}) fusion(f32[256,768]{1,0:T(8,128)S(1)} %copy-done.2, f32[256]{0:T(256)S(1)} %copy-done.23, f32[256]{0:T(256)S(1)} %copy-done.34, bf16[768,1024]{1,0:T(8,128)(2,1)S(1)} %copy-done.40, f32[256,1024]{1,0:T(8,128)S(1)} %get-tuple-element.28, f32[256]{0:T(256)S(1)} %copy-done.37), kind=kOutput, calls=%fused_computation.87 | convolution fusion | flops 419495680 | bytes 3805184 | tf_op jit(solution)/shard_map/transpose(jvp())/dot_general | solution.py:66
  94.1 2.5 %fusion.125 = (f32[256]{0:T(256)S(1)}, f32[256,768]{1,0:T(8,128)S(1)}) fusion(f32[256]{0:T(256)S(1)} %multiply_multiply_fusion.8, bf16[256,768]{1,0:T(8,128)(2,1)S(1)} %get-tuple-element.18, f32[256]{0:T(256)S(1)} %copy-done.34, f32[256,768]{1,0:T(8,128)S(1)} %copy-done.2, f32[256]{0:T(256)S(1)} %copy-done.23), kind=kLoop, calls=%fused_computation.231 | loop fusion | flops 15531776 | bytes 1970176 | tf_op jit(solution)/shard_map/transpose(jvp())/reduce_sum | solution.py:16
  100.4 2.0 %convolution_convert_fusion.2 = bf16[256,1024]{1,0:T(8,128)(2,1)S(1)} fusion(bf16[1024,768]{1,0:T(8,128)(2,1)} %param.15, bf16[256,768]{1,0:T(8,128)(2,1)S(1)} %copy-done.10, bf16[256,768]{1,0:T(8,128)(2,1)S(1)} %copy.90), kind=kOutput, calls=%fused_computation.20 | convolution fusion | flops 403111936 | bytes 2883584 | tf_op jit(solution)/shard_map/transpose(jvp())/dot_general | solution.py:53
  103.3 1.6 %convolution_convert_fusion.16 = bf16[51,1024]{1,0:T(8,128)(2,1)S(1)} fusion(bf16[1024,1024]{1,0:T(8,128)(2,1)S(1)} %copy-done, pred[51,1024]{1,0:T(8,128)(4,1)} %copy-done.13, bf16[51,1024]{1,0:T(8,128)(2,1)S(1)} %gather_fusion.3, pred[51]{0:T(512)(128)(4,1)} %get-tuple-element.4), kind=kOutput, calls=%fused_computation.56 | convolution fusion | flops 107111424 | bytes 2358323 | tf_op jit(solution)/shard_map/transpose(jvp())/dot_general | solution.py:48
  108.7 5.0 %fusion.77 = (f32[51]{0:T(128)S(1)}, f32[51,1024]{1,0:T(8,128)S(1)}) fusion(bf16[51,1024]{1,0:T(8,128)(2,1)S(1)} %gather_fusion.2, f32[51]{0:T(128)S(1)} %copy-done.21, bf16[51,3072]{1,0:T(8,128)(2,1)S(1)} %reshape.268, bf16[1024,3072]{1,0:T(8,128)(2,1)} %param.12), kind=kOutput, calls=%fused_computation.151 | convolution fusion | flops 321177536 | bytes 6918552 | tf_op jit(solution)/shard_map/transpose(jvp())/dot_general | solution.py:46
  114.2 10.2 %all-gather = bf16[4,51,1024]{2,1,0:T(8,128)(2,1)S(1)} all-gather(bf16[1,51,1024]{2,1,0:T(8,128)(2,1)S(1)} %fusion.105), channel_id=1, replica_groups=mesh['dp'=8,'mask'=4] {'mask'}, dimensions={0}, use_global_device_ids=true | all-gather | bytes 522240 | tf_op jit(solution)/shard_map/all_gather | solution.py:132
  (159 shorter events, 29.7 us)
Async XLA Ops:
  7.2 28.1 %copy-start = (bf16[1024,1024]{1,0:T(8,128)(2,1)S(1)}, bf16[1024,1024]{1,0:T(8,128)(2,1)}, u32[]{:S(2)}) copy-start(bf16[1024,1024]{1,0:T(8,128)(2,1)} %param.13) | copy-start | bytes 6291460
  7.2 75.9 %all-reduce.9.cloned.1.call-start = ((), (), s32[]{:S(2)}) async-start(), calls=%async_computation.1 | async-start | bytes 1048576 | tf_op jit(solution)/shard_map/psum | solution.py:114
  35.3 5.4 %copy-start.35 = (s32[4,51]{1,0:T(4,128)S(1)}, s32[4,51]{1,0:T(4,128)}, u32[]{:S(2)}) copy-start(s32[4,51]{1,0:T(4,128)} %param.10) | copy-start | bytes 2452
  37.3 33.3 %all-to-all-start = ((bf16[64,4,192]{2,0,1:T(8,128)(2,1)}), bf16[64,4,192]{2,0,1:T(8,128)(2,1)S(1)}, u32[]{:S(2)}, u32[]{:S(2)}) async-start(bf16[64,4,192]{2,0,1:T(8,128)(2,1)} %copy.73), calls=%async_computation | async-start | bytes 262144 | tf_op jit(solution)/shard_map/all_to_all | solution.py:126
  40.6 11.7 %copy-start.29 = (u32[51]{0:T(128)}, u32[51]{0:T(128)S(1)}, u32[]{:S(2)}) copy-start(u32[51]{0:T(128)S(1)} %iota_add_fusion) | copy-start | bytes 616
  41.9 9.1 %copy-start.28 = (s32[1024]{0:T(1024)}, s32[1024]{0:T(1024)S(1)}, u32[]{:S(2)}) copy-start(s32[1024]{0:T(1024)S(1)} %pad_clamp_fusion) | copy-start | bytes 12292
  42.9 4.3 %copy-start.38 = (f32[51]{0:T(128)}, f32[51]{0:T(128)S(1)}, u32[]{:S(2)}) copy-start(f32[51]{0:T(128)S(1)} %fusion.75) | copy-start | bytes 616
  43.2 4.0 %copy-start.31 = (f32[51]{0:T(128)}, f32[51]{0:T(128)S(1)}, u32[]{:S(2)}) copy-start(f32[51]{0:T(128)S(1)} %fusion.116) | copy-start | bytes 616
  49.9 3.5 %copy-start.36 = (bf16[1024]{0:T(1024)(128)(2,1)S(1)}, bf16[1024]{0:T(1024)(128)(2,1)}, u32[]{:S(2)}) copy-start(bf16[1024]{0:T(1024)(128)(2,1)} %param.14) | copy-start | bytes 6148
  65.5 20.1 %copy-start.18 = (bf16[256,768]{1,0:T(8,128)(2,1)S(1)}, bf16[256,768]{1,0:T(8,128)(2,1)}, u32[]{:S(2)}) copy-start(bf16[256,768]{1,0:T(8,128)(2,1)} %convolution_convert_fusion.7) | copy-start | bytes 1179652
  66.7 19.0 %copy-start.2 = (f32[256,768]{1,0:T(8,128)S(1)}, f32[256,768]{1,0:T(8,128)}, u32[]{:S(2)}) copy-start(f32[256,768]{1,0:T(8,128)} %copy.83) | copy-start | bytes 2359300
  85.6 4.9 %copy-start.23 = (f32[256]{0:T(256)S(1)}, f32[256]{0:T(256)}, u32[]{:S(2)}) copy-start(f32[256]{0:T(256)} %copy-done.22) | copy-start | bytes 3076
  85.6 4.8 %copy-start.34 = (f32[256]{0:T(256)S(1)}, f32[256]{0:T(256)}, u32[]{:S(2)}) copy-start(f32[256]{0:T(256)} %fusion.114) | copy-start | bytes 3076
  85.7 4.8 %copy-start.37 = (f32[256]{0:T(256)S(1)}, f32[256]{0:T(256)}, u32[]{:S(2)}) copy-start(f32[256]{0:T(256)} %get-tuple-element.11) | copy-start | bytes 3076
  85.7 4.8 %copy-start.40 = (bf16[768,1024]{1,0:T(8,128)(2,1)S(1)}, bf16[768,1024]{1,0:T(8,128)(2,1)}, u32[]{:S(2)}) copy-start(bf16[768,1024]{1,0:T(8,128)(2,1)} %param.17) | copy-start | bytes 4718596
  90.5 3.6 %copy-start.25 = (f32[256]{0:T(256)S(1)}, f32[256]{0:T(256)}, u32[]{:S(2)}) copy-start(f32[256]{0:T(256)} %copy-done.24) | copy-start | bytes 3076
  94.0 2.6 %copy-start.9 = (bf16[256,768]{1,0:T(8,128)(2,1)}, bf16[256,768]{1,0:T(8,128)(2,1)S(1)}, u32[]{:S(2)}) copy-start(bf16[256,768]{1,0:T(8,128)(2,1)S(1)} %get-tuple-element.18) | copy-start | bytes 1179652
  96.6 2.1 %copy-start.3 = (bf16[3,16,48,48]{3,2,1,0:T(8,128)(2,1)S(1)}, bf16[3,16,48,48]{3,2,1,0:T(8,128)(2,1)}, u32[]{:S(2)}) copy-start(bf16[3,16,48,48]{3,2,1,0:T(8,128)(2,1)} %param.16) | copy-start | bytes 663556
  108.6 5.1 %copy-start.39 = (f32[51]{0:T(128)S(1)}, f32[51]{0:T(128)}, u32[]{:S(2)}) copy-start(f32[51]{0:T(128)} %copy-done.38) | copy-start | bytes 616
  108.6 5.1 %copy-start.32 = (f32[51]{0:T(128)S(1)}, f32[51]{0:T(128)}, u32[]{:S(2)}) copy-start(f32[51]{0:T(128)} %copy-done.31) | copy-start | bytes 616
  108.7 5.3 %copy-start.4 = (u32[51,1024]{1,0:T(8,128)S(1)}, u32[51,1024]{1,0:T(8,128)}, u32[]{:S(2)}) copy-start(u32[51,1024]{1,0:T(8,128)} %gather_fusion.1) | copy-start | bytes 626692
  108.7 5.3 %copy-start.30 = (u32[51]{0:T(128)S(1)}, u32[51]{0:T(128)}, u32[]{:S(2)}) copy-start(u32[51]{0:T(128)} %copy-done.29) | copy-start | bytes 616
  108.7 5.3 %copy-start.33 = (pred[51]{0:T(512)(128)(4,1)S(1)}, pred[51]{0:T(512)(128)(4,1)}, u32[]{:S(2)}) copy-start(pred[51]{0:T(512)(128)(4,1)} %get-tuple-element.4) | copy-start | bytes 157
  113.7 10.8 %copy-start.16 = (bf16[204,192]{1,0:T(8,128)(2,1)S(1)}, bf16[204,192]{1,0:T(8,128)(2,1)}, u32[]{:S(2)}) copy-start(bf16[204,192]{1,0:T(8,128)(2,1)} %gather_fusion) | copy-start | bytes 235012
  (19 other events, 21.6 us)
Sparse Core Ops, SparseCore 0:
  36.6 46.4 all-reduce.8
where the time goes:
time: 135 us; the launch traced here: 134 us
  matrix products  40.8 us (30%)
  local copies, waits for them, and re-layouts  23.6 us (17%)
  blocking collectives  21.7 us (16%)
  other arithmetic  17.5 us (13%)
  between operations  16.7 us (12%)
  waiting for transfers between devices  10.7 us (8%)
  starting transfers between devices  3.36 us (2%)
    all_gather x1, blocking collectives, on_device(): lax.all_gather(own_embedded, 'mask', axis=0, tiled=True)  11.5 us
    unnamed x84, local copies, waits for them, and re-layouts  11.3 us
    psum x1, waiting for transfers between devices, on_device(): lax.psum(partial_value.astype(jnp.bfloat16), 'mask').astype(jnp.float32)  10.7 us
    all_gather x1, blocking collectives, on_device(): lax.all_gather(grad_in, 'mask', axis=0, tiled=True)  10.2 us
    dot_general x2, matrix products, attention_branch(): jnp.dot(normed, w_qkv, preferred_element_type=jnp.float32)  9 us
    dot_general x2, matrix products, decoder_output(): return jnp.dot(hidden, dec_out, preferred_element_type=jnp.float32)  8.34 us
    dot_general x2, matrix products, decoder_output(): jnp.dot(canvas, dec_in, preferred_element_type=jnp.float32)  4.74 us
    dot_general x6, matrix products, decoder_output(): jnp.einsum('pgi,gio->pgo', padded[offset:offset + total_rows], conv_w[off...  4.62 us
  transfers between devices with their start and end apart: 2, of which 1 were waited for; matrix products, arithmetic and copies ran while one was open for 23% of the time, Pallas kernels for 0%

commit v1 on v0

--- a/solution.py
+++ b/solution.py
@@ -111,7 +111,9 @@
     partial_value = jnp.dot(
         context.reshape(total_rows, head_width), out_rows, preferred_element_type=jnp.float32
     )
-    branch = lax.psum(partial_value.astype(jnp.bfloat16), "mask").astype(jnp.float32)
+    branch = jnp.sum(lax.all_gather(partial_value.astype(jnp.bfloat16), "mask"), axis=0).astype(
+        jnp.float32
+    )
     all_targets = row_norm(branch).astype(jnp.bfloat16)
 
     def objective(rows_in):

time: 135 us -> 125 us (0.926)
  waiting for transfers between devices: 10.7 us -> 0.02 us
  matrix products: 40.8 us -> 42.9 us
  other arithmetic: 17.5 us -> 16.1 us
    psum x1 -> x0, waiting for transfers between devices: 10.7 us -> none  [on_device(): lax.psum(partial_value.astype(jnp.bfloat16), 'mask').astype(jnp.float32)]
    reduce_sum x0 -> x1, other arithmetic: none -> 2.02 us  [on_device(): jnp.sum(lax.all_gather(partial_value.astype(jnp.bfloat16), 'mask'), axis=0)]
    dot_general x6, matrix products: 4.62 us -> 6.14 us  [decoder_output(): jnp.einsum('pgi,gio->pgo', padded[offset:offset + total_rows], conv_w[off...]
    unnamed x84 -> x86, local copies, waits for them, and re-layouts: 11.3 us -> 10.7 us
  transfers between devices with their start and end apart: 2 -> 2, of which waited for: 1 -> 0; matrix products, arithmetic and copies ran while one was open for 23% -> 24% of each run, Pallas kernels for 0% -> 0%
where the time goes in v1:
time: 125 us; the launch traced here: 124 us
  matrix products  42.9 us (34%)
  local copies, waits for them, and re-layouts  23 us (18%)
  blocking collectives  22.4 us (18%)
  between operations  16.6 us (13%)
  other arithmetic  16.1 us (13%)
  starting transfers between devices  3.36 us (3%)
    all_gather x1, blocking collectives, on_device(): lax.all_gather(own_embedded, 'mask', axis=0, tiled=True)  11.5 us
    all_gather x1, blocking collectives, on_device(): lax.all_gather(grad_in, 'mask', axis=0, tiled=True)  10.8 us
    unnamed x86, local copies, waits for them, and re-layouts  10.7 us
    dot_general x2, matrix products, attention_branch(): jnp.dot(normed, w_qkv, preferred_element_type=jnp.float32)  9.35 us
    dot_general x2, matrix products, decoder_output(): return jnp.dot(hidden, dec_out, preferred_element_type=jnp.float32)  8.2 us
    dot_general x6, matrix products, decoder_output(): jnp.einsum('pgi,gio->pgo', padded[offset:offset + total_rows], conv_w[off...  6.14 us
    dot_general x2, matrix products, decoder_output(): jnp.dot(canvas, dec_in, preferred_element_type=jnp.float32)  4.89 us
    dot_general x4, matrix products, mix_heads(): jnp.einsum('hqk,khd->qhd', weights, values, preferred_element_type=jnp.fl...  3.84 us
  transfers between devices with their start and end apart: 2, of which 0 were waited for; matrix products, arithmetic and copies ran while one was open for 24% of the time, Pallas kernels for 0%

profile of v1, /device:TPU:0, one launch (start us, length us, event | category | flops | bytes accessed | tf_op | source)
XLA Modules:
  0.0 124.4 jit_solution(12562598091952762614)
XLA Ops:
  7.2 2.0 %convolution_convert_fusion.14 = bf16[64,1024]{1,0:T(8,128)(2,1)S(1)} fusion(bf16[64,768]{1,0:T(8,128)(2,1)} %param.9, bf16[768,1024]{1,0:T(8,128)(2,1)} %param.11), kind=kOutput, calls=%fused_computation.52 | convolution fusion | flops 100728832 | bytes 1802240 | tf_op jit(solution)/shard_map/dot_general | solution.py:94
  9.2 11.5 %all_gather.12 = bf16[256,1024]{1,0:T(8,128)(2,1)S(1)} all-gather(bf16[64,1024]{1,0:T(8,128)(2,1)S(1)} %convolution_convert_fusion.14), channel_id=1, replica_groups=mesh['dp'=8,'mask'=4] {'mask'}, dimensions={0}, use_global_device_ids=true | all-gather | bytes 655360 | tf_op jit(solution)/shard_map/all_gather | solution.py:98
  21.2 8.7 %copy.84 = bf16[1024,3072]{0,1:T(8,128)(2,1)} copy(bf16[1024,3072]{1,0:T(8,128)(2,1)} %param.12) | data formatting | bytes 12582912 | tf_op args[3]
  29.9 2.1 %fusion.4 = bf16[256,3,256]{0,2,1:T(8,128)(2,1)S(1)} fusion(bf16[1024,3,1024]{0,2,1:T(8,128)(2,1)} %bitcast.174, s32[]{:T(128)S(6)} %select_n.51, bf16[256,1024]{1,0:T(8,128)(2,1)S(1)} %all_gather.12, f32[256]{0:T(256)S(1)} %add_rsqrt_fusion.3, f32[256]{0:T(256)S(1)} %broadcast_multiply_fusion.2), kind=kOutput, calls=%fused_computation.21 | convolution fusion | flops 403898368 | bytes 2492420 | tf_op jit(solution)/shard_map/sd,dtw->stw/dot_general | solution.py:106
  32.1 1.3 %fusion.2 = f32[4,256,256]{1,2,0:T(8,128)} fusion(f32[256,4]{0,1:T(4,128)S(1)} %get-tuple-element.31, f32[256,4]{0,1:T(4,128)S(1)} %get-tuple-element.32, bf16[256,3,4,64]{0,3,2,1:T(8,128)(2,1)S(1)} %bitcast.184), kind=kOutput, calls=%fused_computation.10 | convolution fusion | flops 34209792 | bytes 1318912 | tf_op jit(solution)/shard_map/qhd,khd->hqk/dot_general | solution.py:28
  33.4 1.9 %convolution_convert_fusion.13 = bf16[4,64,256]{2,1,0:T(8,128)(2,1)S(1)} fusion(f32[4,256,256]{1,2,0:T(8,128)} %fusion.2, bf16[256,3,4,64]{0,3,2,1:T(8,128)(2,1)S(1)} %bitcast.185), kind=kOutput, calls=%fused_computation.51 | convolution fusion | flops 34145536 | bytes 2359296 | tf_op jit(solution)/shard_map/hqk,khd->qhd/dot_general | solution.py:33
  37.3 3.3 %all-to-all-start = ((bf16[64,4,192]{2,0,1:T(8,128)(2,1)}), bf16[64,4,192]{2,0,1:T(8,128)(2,1)S(1)}, u32[]{:S(2)}, u32[]{:S(2)}) async-start(bf16[64,4,192]{2,0,1:T(8,128)(2,1)} %copy.73), calls=%async_computation | async-start | bytes 262144 | tf_op jit(solution)/shard_map/all_to_all | solution.py:128
  42.7 4.4 %convolution_convert_fusion = bf16[51,3072]{1,0:T(8,128)(2,1)S(1)} fusion(bf16[1024,3072]{1,0:T(8,128)(2,1)} %param.12, bf16[51,1024]{1,0:T(8,128)(2,1)S(1)} %gather_fusion.2, f32[51]{0:T(128)S(1)} %fusion.116, f32[51]{0:T(128)S(1)} %broadcast_multiply_fusion.4), kind=kOutput, calls=%fused_computation.6 | convolution fusion | flops 321229824 | bytes 6709656 | tf_op jit(solution)/shard_map/jvp()/dot_general | solution.py:46
  51.1 1.3 %gather_fusion.1 = u32[51,1024]{1,0:T(8,128)} fusion(u32[256,1024]{1,0:T(8,128)S(1)} %scatter_custom_fusion, s32[1024]{0:T(1024)S(1)} %pad_clamp_fusion), kind=kCustom, calls=%fused_computation.1 | custom fusion | bytes 417996 | tf_op jit(solution)/shard_map/jvp()/gather | solution.py:52
  55.6 1.5 %scatter_fusion = bf16[256,1024]{1,0:T(8,128)(2,1)S(1)} fusion(bf16[256,1024]{1,0:T(8,128)(2,1)S(1)} %copy-done.1, s32[51]{0:T(128)S(1)} %fusion.115, bf16[51,1024]{1,0:T(8,128)(2,1)S(1)} %fusion.24), kind=kCustom, calls=%fused_computation.5 | custom fusion | flops 52224 | bytes 313548 | tf_op jit(solution)/shard_map/jvp()/scatter-add | solution.py:52
  57.1 2.7 %convolution_convert_fusion.7 = bf16[256,768]{1,0:T(8,128)(2,1)} fusion(bf16[256,1024]{1,0:T(8,128)(2,1)S(1)} %scatter_fusion, bf16[1024,768]{1,0:T(8,128)(2,1)} %param.15), kind=kOutput, calls=%fused_computation.26 | convolution fusion | flops 402849792 | bytes 2490368 | tf_op jit(solution)/shard_map/jvp()/dot_general | solution.py:53
  61.0 1.3 %fusion.62 = f32[16,256,48]{1,2,0:T(8,128)S(1)} fusion(bf16[256,16,48]{0,2,1:T(8,128)(2,1)S(1)} %bitcast.178, bf16[3,16,48,48]{3,2,1,0:T(8,128)(2,1)} %param.16), kind=kOutput, calls=%fused_computation.126 | convolution fusion | flops 18874368 | bytes 1376256 | tf_op jit(solution)/shard_map/jvp(pgi,gio->pgo)/dot_general | solution.py:58
  62.4 1.2 convolution_add_fusion.1
  63.6 1.9 %fusion.128 = (f32[256]{0:T(256)}, f32[16,256,48]{1,2,0:T(8,128)S(1)}) fusion(f32[16,256,48]{1,2,0:T(8,128)S(1)} %convolution_add_fusion.1, bf16[256,16,48]{0,2,1:T(8,128)(2,1)S(1)} %bitcast.180, bf16[3,16,48,48]{3,2,1,0:T(8,128)(2,1)} %param.16), kind=kOutput, calls=%fused_computation.234 | convolution fusion | flops 19267328 | bytes 2163712 | tf_op jit(solution)/shard_map/jvp(pgi,gio->pgo)/dot_general | solution.py:58
  66.7 1.2 compare_and_fusion
  70.6 1.7 %gather_fusion = bf16[204,192]{1,0:T(8,128)(2,1)} fusion(bf16[256,192]{1,0:T(8,128)(2,1)S(1)} %bitcast.172, s32[1024]{0:T(1024)S(1)} %pad_clamp_fusion.1), kind=kCustom, calls=%fused_computation | custom fusion | bytes 157488 | tf_op jit(solution)/shard_map/gather | solution.py:130
  72.3 2.0 %reduce_sum.250 = bf16[256,1024]{1,0:T(8,128)(2,1)S(1)} reduce(bf16[4,256,1024]{2,1,0:T(8,128)(2,1)} %bitcast.181, bf16[]{:T(256)} %constant.56.clone.1), dimensions={0}, to_apply=%region_14.15 | reduce | flops 786432 | bytes 2621442 | tf_op jit(solution)/shard_map/reduce_sum | solution.py:114
  74.8 4.7 %multiply_reduce_fusion = (f32[]{:T(128)}, f32[256,1024]{1,0:T(8,128)S(1)}) fusion(f32[256]{0:T(256)} %get-tuple-element.12, f32[256]{0:T(256)S(1)} %add_rsqrt_fusion.2, f32[256]{0:T(256)S(1)} %broadcast_multiply_fusion.1, bf16[256,1024]{1,0:T(8,128)(2,1)S(1)} %reduce_sum.250, bf16[768,1024]{1,0:T(8,128)(2,1)} %param.17, ...), kind=kOutput, calls=%fused_computation.64 | convolution fusion | flops 418971648 | bytes 4330500 | tf_op jit(solution)/shard_map/jvp()/dot_general | solution.py:66
  79.5 3.5 %multiply_reduce_fusion.1 = (f32[256]{0:T(256)S(1)}, bf16[256,768]{1,0:T(8,128)(2,1)S(1)}) fusion(f32[256,768]{1,0:T(8,128)S(1)} %copy-done.2, f32[256]{0:T(256)S(1)} %copy-done.22, f32[256]{0:T(256)S(1)} %copy-done.34, bf16[768,1024]{1,0:T(8,128)(2,1)S(1)} %copy-done.41, f32[256,1024]{1,0:T(8,128)S(1)} %get-tuple-element.28, f32[256]{0:T(256)S(1)} %copy-done.38), kind=kOutput, calls=%fused_computation.87 | convolution fusion | flops 419495680 | bytes 3805184 | tf_op jit(solution)/shard_map/transpose(jvp())/dot_general | solution.py:66
  83.1 2.5 %fusion.125 = (f32[256]{0:T(256)S(1)}, f32[256,768]{1,0:T(8,128)S(1)}) fusion(f32[256]{0:T(256)S(1)} %multiply_multiply_fusion.8, bf16[256,768]{1,0:T(8,128)(2,1)S(1)} %get-tuple-element.18, f32[256]{0:T(256)S(1)} %copy-done.34, f32[256,768]{1,0:T(8,128)S(1)} %copy-done.2, f32[256]{0:T(256)S(1)} %copy-done.22), kind=kLoop, calls=%fused_computation.231 | loop fusion | flops 15531776 | bytes 1970176 | tf_op jit(solution)/shard_map/transpose(jvp())/reduce_sum | solution.py:16
  89.9 2.2 %convolution_convert_fusion.2 = bf16[256,1024]{1,0:T(8,128)(2,1)S(1)} fusion(bf16[1024,768]{1,0:T(8,128)(2,1)} %param.15, bf16[256,768]{1,0:T(8,128)(2,1)} %copy-done.9, bf16[256,768]{1,0:T(8,128)(2,1)S(1)} %copy.90), kind=kOutput, calls=%fused_computation.20 | convolution fusion | flops 403111936 | bytes 2883584 | tf_op jit(solution)/shard_map/transpose(jvp())/dot_general | solution.py:53
  94.0 1.3 %fusion.21 = bf16[51,1,16,64]{3,0,2,1:T(8,128)(2,1)S(1)} fusion(bf16[51,16,64]{2,1,0:T(8,128)(2,1)S(1)} %reshape.267, f32[16,51,51]{1,2,0:T(8,128)} %copy-done.14, f32[16,51]{1,0:T(8,128)S(1)} %copy-done.27), kind=kOutput, calls=%fused_computation.49 | convolution fusion | flops 5462304 | bytes 378624 | tf_op jit(solution)/shard_map/transpose(jvp(hqk,khd->qhd))/dot_general | solution.py:33
  98.2 5.0 %fusion.77 = (f32[51]{0:T(128)S(1)}, f32[51,1024]{1,0:T(8,128)S(1)}) fusion(bf16[51,1024]{1,0:T(8,128)(2,1)S(1)} %gather_fusion.2, f32[51]{0:T(128)S(1)} %copy-done.20, bf16[51,3072]{1,0:T(8,128)(2,1)S(1)} %reshape.268, bf16[1024,3072]{1,0:T(8,128)(2,1)} %param.12), kind=kOutput, calls=%fused_computation.151 | convolution fusion | flops 321177536 | bytes 6918552 | tf_op jit(solution)/shard_map/transpose(jvp())/dot_general | solution.py:46
  103.7 10.8 %all-gather.1 = bf16[4,51,1024]{2,1,0:T(8,128)(2,1)S(1)} all-gather(bf16[1,51,1024]{2,1,0:T(8,128)(2,1)S(1)} %fusion.105), channel_id=1, replica_groups=mesh['dp'=8,'mask'=4] {'mask'}, dimensions={0}, use_global_device_ids=true | all-gather | bytes 522240 | tf_op jit(solution)/shard_map/all_gather | solution.py:134
  (162 shorter events, 27.6 us)
Async XLA Ops:
  7.2 28.1 %copy-start = (bf16[1024,1024]{1,0:T(8,128)(2,1)S(1)}, bf16[1024,1024]{1,0:T(8,128)(2,1)}, u32[]{:S(2)}) copy-start(bf16[1024,1024]{1,0:T(8,128)(2,1)} %param.13) | copy-start | bytes 6291460
  7.2 65.1 %all-gather.4.cloned.1.call-start = ((), (), s32[]{:S(2)}) async-start(), calls=%async_computation.1 | async-start | bytes 2621440 | tf_op jit(solution)/shard_map/all_gather | solution.py:114
  35.3 5.4 %copy-start.36 = (s32[4,51]{1,0:T(4,128)S(1)}, s32[4,51]{1,0:T(4,128)}, u32[]{:S(2)}) copy-start(s32[4,51]{1,0:T(4,128)} %param.10) | copy-start | bytes 2452
  37.3 33.3 %all-to-all-start = ((bf16[64,4,192]{2,0,1:T(8,128)(2,1)}), bf16[64,4,192]{2,0,1:T(8,128)(2,1)S(1)}, u32[]{:S(2)}, u32[]{:S(2)}) async-start(bf16[64,4,192]{2,0,1:T(8,128)(2,1)} %copy.73), calls=%async_computation | async-start | bytes 262144 | tf_op jit(solution)/shard_map/all_to_all | solution.py:128
  40.6 12.7 %copy-start.29 = (u32[51]{0:T(128)}, u32[51]{0:T(128)S(1)}, u32[]{:S(2)}) copy-start(u32[51]{0:T(128)S(1)} %iota_add_fusion) | copy-start | bytes 616
  41.3 9.8 %copy-start.28 = (s32[1024]{0:T(1024)}, s32[1024]{0:T(1024)S(1)}, u32[]{:S(2)}) copy-start(s32[1024]{0:T(1024)S(1)} %pad_clamp_fusion) | copy-start | bytes 12292
  42.4 4.7 %copy-start.39 = (f32[51]{0:T(128)}, f32[51]{0:T(128)S(1)}, u32[]{:S(2)}) copy-start(f32[51]{0:T(128)S(1)} %fusion.75) | copy-start | bytes 616
  42.7 4.4 %copy-start.31 = (f32[51]{0:T(128)}, f32[51]{0:T(128)S(1)}, u32[]{:S(2)}) copy-start(f32[51]{0:T(128)S(1)} %fusion.116) | copy-start | bytes 616
  65.5 3.8 %copy-start.35 = (s32[204,1]{0,1:T(1,128)S(1)}, s32[204,1]{0,1:T(1,128)}, u32[]{:S(2)}) copy-start(s32[204,1]{0,1:T(1,128)} %reshape.257) | copy-start | bytes 2452
  65.6 4.4 %copy-start.26 = (f32[16,51]{1,0:T(8,128)S(1)}, f32[16,51]{1,0:T(8,128)}, u32[]{:S(2)}) copy-start(f32[16,51]{1,0:T(8,128)} %copy-done.25) | copy-start | bytes 9796
  70.6 4.2 %copy-start.2 = (f32[256,768]{1,0:T(8,128)S(1)}, f32[256,768]{1,0:T(8,128)}, u32[]{:S(2)}) copy-start(f32[256,768]{1,0:T(8,128)} %copy.83) | copy-start | bytes 2359300
  74.8 4.7 %copy-start.22 = (f32[256]{0:T(256)S(1)}, f32[256]{0:T(256)}, u32[]{:S(2)}) copy-start(f32[256]{0:T(256)} %copy-done.21) | copy-start | bytes 3076
  74.8 4.7 %copy-start.34 = (f32[256]{0:T(256)S(1)}, f32[256]{0:T(256)}, u32[]{:S(2)}) copy-start(f32[256]{0:T(256)} %fusion.114) | copy-start | bytes 3076
  74.8 4.7 %copy-start.38 = (f32[256]{0:T(256)S(1)}, f32[256]{0:T(256)}, u32[]{:S(2)}) copy-start(f32[256]{0:T(256)} %get-tuple-element.11) | copy-start | bytes 3076
  74.8 4.7 %copy-start.41 = (bf16[768,1024]{1,0:T(8,128)(2,1)S(1)}, bf16[768,1024]{1,0:T(8,128)(2,1)}, u32[]{:S(2)}) copy-start(bf16[768,1024]{1,0:T(8,128)(2,1)} %param.17) | copy-start | bytes 4718596
  79.5 3.5 %copy-start.24 = (f32[256]{0:T(256)S(1)}, f32[256]{0:T(256)}, u32[]{:S(2)}) copy-start(f32[256]{0:T(256)} %copy-done.23) | copy-start | bytes 3076
  85.6 3.2 %copy-start.3 = (bf16[3,16,48,48]{3,2,1,0:T(8,128)(2,1)S(1)}, bf16[3,16,48,48]{3,2,1,0:T(8,128)(2,1)}, u32[]{:S(2)}) copy-start(bf16[3,16,48,48]{3,2,1,0:T(8,128)(2,1)} %param.16) | copy-start | bytes 663556
  89.9 3.1 %copy-start.13 = (pred[51,1024]{1,0:T(8,128)(4,1)S(1)}, pred[51,1024]{1,0:T(8,128)(4,1)}, u32[]{:S(2)}) copy-start(pred[51,1024]{1,0:T(8,128)(4,1)} %copy-done.12) | copy-start | bytes 156676
  89.9 3.1 %copy-start.33 = (pred[51]{0:T(512)(128)(4,1)S(1)}, pred[51]{0:T(512)(128)(4,1)}, u32[]{:S(2)}) copy-start(pred[51]{0:T(512)(128)(4,1)} %get-tuple-element.4) | copy-start | bytes 157
  98.2 5.0 %copy-start.40 = (f32[51]{0:T(128)S(1)}, f32[51]{0:T(128)}, u32[]{:S(2)}) copy-start(f32[51]{0:T(128)} %copy-done.39) | copy-start | bytes 616
  98.2 5.0 %copy-start.32 = (f32[51]{0:T(128)S(1)}, f32[51]{0:T(128)}, u32[]{:S(2)}) copy-start(f32[51]{0:T(128)} %copy-done.31) | copy-start | bytes 616
  98.2 5.3 %copy-start.4 = (u32[51,1024]{1,0:T(8,128)S(1)}, u32[51,1024]{1,0:T(8,128)}, u32[]{:S(2)}) copy-start(u32[51,1024]{1,0:T(8,128)} %gather_fusion.1) | copy-start | bytes 626692
  98.2 5.3 %copy-start.30 = (u32[51]{0:T(128)S(1)}, u32[51]{0:T(128)}, u32[]{:S(2)}) copy-start(u32[51]{0:T(128)} %copy-done.29) | copy-start | bytes 616
  103.2 11.5 %copy-start.16 = (bf16[204,192]{1,0:T(8,128)(2,1)S(1)}, bf16[204,192]{1,0:T(8,128)(2,1)}, u32[]{:S(2)}) copy-start(bf16[204,192]{1,0:T(8,128)(2,1)} %gather_fusion) | copy-start | bytes 235012
  (20 other events, 33.1 us)
Sparse Core Ops, SparseCore 0:
  36.6 35.5 all-gather.3
